TPU v7x, 256 devices: a whole 4x4x8 slice. The times are simulated.
256 devices in a mesh: req: 64 (over z, x, core), kv: 4 (over y).
Axes of the slice: x: 4, y: 4, z: 8, core: 2. Of those that a mesh axis runs over, the one named last changes fastest.
Arguments:
- residual_in: bfloat16 [128, 2560], P('req', 'kv'), may hold values from -8 to 8
- queries: bfloat16 [128, 2560], P('req', 'kv'), may hold values from -480 to 480
- fresh_token_keys: bfloat16 [128, 512], P('req', 'kv'), may hold values from -6 to 6
- fresh_token_values: bfloat16 [128, 512], P('req', 'kv'), may hold values from -6 to 6
- cached_key_slots: bfloat16 [128, 4096, 512], P('req', None, 'kv'), may hold values from -6 to 6
- cached_value_slots: bfloat16 [128, 4096, 512], P('req', None, 'kv'), may hold values from -6 to 6
- lengths: int32 [128], replicated, may hold values from 1 to 4096, as said below
- slot_order: int32 [128], replicated, may hold values from 0 to 127, as said below
- out_proj: bfloat16 [2560, 2560], P('kv'), may hold values from -0.5 to 0.5
- norm_gain: bfloat16 [2560], P('kv'), may hold values from 0.5 to 1.5
- expert_ids: int32 [128, 6], replicated, may hold values from 0 to 63, all different within a row; in each aligned block of 128 rows (0 to 127, 128 to 255, ...) at most 24 rows name the same one
- gate_values: float32 [128, 6], replicated, may hold values from 0.1 to 0.5
- gate_proj: bfloat16 [64, 2560, 1536], P('req', None, 'kv'), may hold values from -0.125 to 0.125
- up_proj: bfloat16 [64, 2560, 1536], P('req', None, 'kv'), may hold values from -0.125 to 0.125
- down_proj: bfloat16 [64, 1536, 2560], P('req', 'kv'), may hold values from -0.15625 to 0.15625
Outputs:
- layer_out: bfloat16 [128, 2560], P('req', 'kv')
Inputs may be any that keep to these rules, and one draw needn't show every extreme that they name: `lengths`: each request's count of cached positions; some request has exactly 4096. A permutation of the requests: slot s serves request slot_order[s], and cached_key_slots[s], cached_value_slots[s] hold that request's cache. Requests sorted by decreasing length are dealt to the 64 groups of 2 consecutive slots, one round forward, the next backward. `expert_ids`: each token names 6 different experts; no expert is named by more than 24 tokens, a bound that some block reaches.
All inputs are finite; a program needn't handle non-finite values.
Results may differ from a plain program's by a relative error of at most 0.012.
Values may be sent and summed in bfloat16 or wider, within the bound.
No kernel may reach another device: no remote copies, remote signals or barrier semaphores. Data moves between devices by JAX's collectives and lax.ppermute only.
A program may use at most 64 MiB of HBM per device.

v0:
```python
import math
import jax
import jax.numpy as jnp
from jax import lax
from jax.sharding import PartitionSpec as P

COMBINE = "a2a"


def per_device(
    residual_in,
    queries,
    fresh_token_keys,
    fresh_token_values,
    cached_key_slots,
    cached_value_slots,
    lengths,
    slot_order,
    out_proj,
    norm_gain,
    expert_ids,
    gate_values,
    gate_proj,
    up_proj,
    down_proj,
):
    req_count = lax.axis_size("req")
    kv_count = lax.axis_size("kv")
    req_index = lax.axis_index("req")
    kv_index = lax.axis_index("kv")
    per_dev = residual_in.shape[0]
    head_dim = fresh_token_keys.shape[1]
    col_count = residual_in.shape[1]
    total_reqs = lengths.shape[0]
    model_width = out_proj.shape[1]
    q_width = queries.shape[1]
    packed = jnp.concatenate([queries, fresh_token_keys, fresh_token_values, residual_in], axis=1)
    all_packed = lax.all_gather(packed, "req", axis=0, tiled=True)
    served = lax.dynamic_slice_in_dim(slot_order, req_index * per_dev, per_dev)
    mine = all_packed[served]
    query_rows = mine[:, :q_width].reshape(per_dev, -1, head_dim)
    self_key_row = mine[:, q_width : q_width + head_dim]
    self_value_row = mine[:, q_width + head_dim : q_width + 2 * head_dim]
    residual_rows = mine[:, q_width + 2 * head_dim :]
    live_len = lengths[served]
    inv_root = 1.0 / math.sqrt(head_dim)
    scores = (
        jnp.einsum("rqd,rld->rql", query_rows, cached_key_slots, preferred_element_type=jnp.float32)
        * inv_root
    )
    positions = jnp.arange(cached_key_slots.shape[1])
    scores = jnp.where((positions[None, :] < live_len[:, None])[:, None, :], scores, -1e30)
    own_score = (
        jnp.einsum("rqd,rd->rq", query_rows, self_key_row, preferred_element_type=jnp.float32)
        * inv_root
    )
    highest = jnp.maximum(jnp.max(scores, axis=2), own_score)
    weights = jnp.exp(scores - highest[:, :, None])
    own_weight = jnp.exp(own_score - highest)
    totals = jnp.sum(weights, axis=2) + own_weight
    numerator = jnp.einsum(
        "rql,rld->rqd",
        weights.astype(jnp.bfloat16),
        cached_value_slots,
        preferred_element_type=jnp.float32,
    )
    own_low = lax.optimization_barrier(own_weight.astype(jnp.bfloat16)).astype(jnp.float32)
    numerator = numerator + own_low[:, :, None] * self_value_row.astype(jnp.float32)[:, None, :]
    attended = (numerator / totals[:, :, None]).astype(jnp.bfloat16).reshape(per_dev, -1)
    projected = jnp.dot(attended, out_proj, preferred_element_type=jnp.float32)
    col_start = kv_index * col_count
    own_cols = jnp.concatenate(
        [residual_rows.astype(jnp.float32), norm_gain.astype(jnp.float32)[None, :]], axis=0
    )
    summed_in = jnp.concatenate(
        [projected, jnp.zeros((1, model_width), jnp.float32)], axis=0
    ) + lax.dynamic_update_slice(
        jnp.zeros((per_dev + 1, model_width), jnp.float32), own_cols, (0, col_start)
    )
    summed = lax.psum(summed_in, "kv")
    hidden = summed[:per_dev]
    gain = summed[per_dev]
    squares = jnp.sum(hidden * hidden, axis=1)
    normed = (hidden * lax.rsqrt(squares / model_width + 1e-06)[:, None] * gain).astype(
        jnp.bfloat16
    )
    by_slot = lax.all_gather(normed, "req", axis=0, tiled=True)
    slot_of = (
        jnp.zeros((total_reqs,), jnp.int32)
        .at[slot_order]
        .set(jnp.arange(total_reqs, dtype=jnp.int32))
    )
    local_count = gate_proj.shape[0]
    capacity = min(2 * total_reqs * expert_ids.shape[1] // (local_count * req_count), total_reqs)
    expert = req_index * local_count + 0
    named_here = expert_ids == expert
    token_gate = jnp.sum(jnp.where(named_here, gate_values, 0.0), axis=1)
    uses_expert = jnp.any(named_here, axis=1)
    picked = jnp.nonzero(uses_expert, size=capacity, fill_value=0)[0].astype(jnp.int32)
    valid_rows = jnp.arange(capacity) < jnp.sum(uses_expert.astype(jnp.int32))
    row_block = by_slot[slot_of[picked]]
    gate_h = jnp.dot(row_block, gate_proj[0], preferred_element_type=jnp.float32)
    up_h = jnp.dot(row_block, up_proj[0], preferred_element_type=jnp.float32)
    inner_act = (jax.nn.silu(gate_h) * up_h).astype(jnp.bfloat16)
    outputs = jnp.dot(inner_act, down_proj[0], preferred_element_type=jnp.float32)
    row_gate = jnp.where(valid_rows, token_gate[picked], 0.0)
    weighted = outputs * row_gate[:, None]
    weighted = lax.psum_scatter(weighted, "kv", scatter_dimension=1, tiled=True)
    own_hidden = lax.dynamic_slice_in_dim(hidden, col_start, col_count, axis=1)
    combined = (
        jnp.zeros((total_reqs, col_count), jnp.float32)
        .at[picked]
        .add(weighted)
        .at[served]
        .add(own_hidden)
    )
    if COMBINE == "rs":
        layer_rows = lax.psum_scatter(combined, "req", scatter_dimension=0, tiled=True)
    else:
        layer_rows = jnp.sum(
            lax.all_to_all(
                combined.reshape(req_count, per_dev, col_count), "req", 0, 0, tiled=False
            ),
            axis=0,
        )
    return layer_rows.astype(jnp.bfloat16)


def solution(mesh):
    in_specs = (
        P("req", "kv"),
        P("req", "kv"),
        P("req", "kv"),
        P("req", "kv"),
        P("req", None, "kv"),
        P("req", None, "kv"),
        P(),
        P(),
        P("kv", None),
        P("kv"),
        P(),
        P(),
        P("req", None, "kv"),
        P("req", None, "kv"),
        P("req", "kv", None),
    )
    out_specs = P("req", "kv")
    return jax.shard_map(
        per_device, mesh=mesh, in_specs=in_specs, out_specs=out_specs, check_vma=False
    )
```

profile of v0, /device:TPU:1, one launch (start us, length us, event | category | flops | bytes accessed | tf_op | source)
XLA Modules:
  0.0 225.2 jit_solution(8981033612592452208)
XLA Ops:
  6.5 0.9 compare_select_fusion.4
  8.0 0.7 maximum_bitcast_fusion
  8.7 57.9 %all-gather = bf16[64,2,1536]{2,1,0:T(2,128)(2,1)} all-gather(bf16[1,2,1536]{2,1,0:T(2,128)(2,1)S(1)} %maximum_bitcast_fusion), channel_id=1, replica_groups=mesh['req'=64,'kv'=4] {'req'}, dimensions={0}, use_global_device_ids=true | all-gather | bytes 399360 | tf_op jit(solution)/shard_map/all_gather | solution.py:38
  66.6 1.9 reshape.232
  68.5 1.6 gather_fusion.1
  70.2 1.3 gather_fusion
  71.7 2.3 %fusion.51 = (f32[2,5]{1,0:T(2,128)S(1)}, f32[2,5,4096]{2,1,0:T(8,128)S(1)}) fusion(bf16[2,5,128]{2,1,0:T(8,128)(2,1)S(1)} %reshape.151, bf16[2,4096,128]{2,1,0:T(8,128)(2,1)} %param.19, pred[2,4096]{1,0:T(4,128)(4,1)S(1)} %iota_compare_fusion), kind=kOutput, calls=%fused_computation.85 | convolution fusion | flops 10608630 | bytes 2271784 | tf_op jit(solution)/shard_map/rqd,rld->rql/dot_general | solution.py:48
  76.1 2.0 fusion.16
  78.8 13.9 %psum.7 = f32[3,2560]{1,0:T(4,128)S(1)} all-reduce(f32[3,2560]{1,0:T(4,128)S(1)} %add_dynamic-update-slice_fusion), channel_id=1, replica_groups=mesh['req'=64,'kv'=4] {'kv'}, use_global_device_ids=true, to_apply=%region_7.8 | all-reduce | flops 7680 | bytes 61440 | tf_op jit(solution)/shard_map/psum | solution.py:80
  93.6 56.6 %all-gather.1 = bf16[64,2,2560]{2,1,0:T(2,128)(2,1)} all-gather(bf16[1,2,2560]{2,1,0:T(2,128)(2,1)S(1)} %fusion.34), channel_id=1, replica_groups=mesh['req'=64,'kv'=4] {'req'}, dimensions={0}, use_global_device_ids=true | all-gather | bytes 665600 | tf_op jit(solution)/shard_map/all_gather | solution.py:87
  150.2 2.7 %reshape.234 = bf16[128,2560]{1,0:T(8,128)(2,1)} reshape(bf16[64,2,2560]{2,1,0:T(2,128)(2,1)} %all-gather.1) | data formatting | bytes 1310720
  153.3 1.4 scatter_custom_fusion
  154.9 0.8 fusion.32
  155.6 1.0 scatter_custom_fusion.1
  157.5 0.7 gather_fusion.4
  158.9 1.9 gather_fusion.3
  160.8 1.9 fusion.4
  162.8 3.8 %convolution_multiply_fusion.1 = f32[24,2560]{1,0:T(8,128)} fusion(bf16[1,384,2560]{2,1,0:T(8,128)(2,1)} %param.29, bf16[24,2560]{1,0:T(8,128)(2,1)S(1)} %gather_fusion.3, bf16[1,2560,384]{2,1,0:T(8,128)(2,1)} %param.28, f32[24]{0:T(128)S(1)} %compare_select_fusion.5, f32[24,384]{1,0:T(8,128)S(1)} %fusion.4), kind=kOutput, calls=%fused_computation.11 | convolution fusion | flops 94488576 | bytes 4337760 | tf_op jit(solution)/shard_map/dot_general | solution.py:105
  166.5 16.9 %reduce-scatter.2.cloned.1.call-done = f32[24,640]{1,0:T(8,128)} async-done(((f32[24,2560]{1,0:T(8,128)}), f32[24,640]{1,0:T(8,128)}) %reduce-scatter.2.cloned.1.call-update) | async-done | bytes 61456 | tf_op jit(solution)/shard_map/reduce_scatter | solution.py:108
  183.5 1.7 scatter_custom_fusion.2
  185.2 2.4 %scatter_custom_fusion.3 = f32[128,640]{1,0:T(8,128)} fusion(f32[128,640]{1,0:T(8,128)} %scatter_custom_fusion.2, s32[2]{0:T(128)} %copy-done.3, f32[2,2560]{1,0:T(2,128)S(1)} %get-tuple-element.7, s32[]{:T(128)} %constant.31.clone.1, s32[]{:T(128)S(6)} %select_n.104), kind=kCustom, calls=%fused_computation.54 | custom fusion | flops 1280 | bytes 333316 | tf_op jit(solution)/shard_map/scatter-add | solution.py:115
  187.6 1.9 reshape.153
  189.5 27.2 %all_to_all.5 = f32[64,2,640]{2,1,0:T(2,128)} all-to-all(f32[64,2,640]{2,1,0:T(2,128)} %reshape.153), channel_id=1, replica_groups=mesh['req'=64,'kv'=4] {'req'}, dimensions={0} | all-to-all | bytes 655360 | tf_op jit(solution)/shard_map/all_to_all | solution.py:121
  216.7 1.7 reduce_sum.53
  (47 shorter events, 6.5 us)
Async XLA Ops:
  6.5 71.6 %copy-start = (bf16[640,2560]{1,0:T(8,128)(2,1)S(1)}, bf16[640,2560]{1,0:T(8,128)(2,1)}, u32[]{:S(2)}) copy-start(bf16[640,2560]{1,0:T(8,128)(2,1)} %param.23) | copy-start | bytes 9830404
  6.5 176.9 %reduce-scatter.2.cloned.1.call-start = ((), (), s32[]{:S(2)}) async-start(), calls=%async_computation.2 | async-start | bytes 307200 | tf_op jit(solution)/shard_map/reduce_scatter | solution.py:108
  7.4 0.5 copy-start.3
  78.1 14.7 %copy-start.1 = (f32[128,6]{0,1:T(8,128)S(1)}, f32[128,6]{0,1:T(8,128)}, u32[]{:S(2)}) copy-start(f32[128,6]{0,1:T(8,128)} %param.26) | copy-start | bytes 9220
  78.1 14.7 %copy-start.2 = (s32[128,6]{0,1:T(8,128)S(1)}, s32[128,6]{0,1:T(8,128)}, u32[]{:S(2)}) copy-start(s32[128,6]{0,1:T(8,128)} %param.25) | copy-start | bytes 9220
  78.2 14.7 %copy-start.4 = (s32[128]{0:T(128)S(1)}, s32[128]{0:T(128)}, u32[]{:S(2)}) copy-start(s32[128]{0:T(128)} %param.22) | copy-start | bytes 1540
Sparse Core Ops, SparseCore 0:
  166.7 16.7 reduce-scatter.1
where the time goes:
time: 226 us; the launch traced here: 225 us
  blocking collectives  156 us (69%)
  waiting for transfers between devices  17 us (8%)
  local copies, waits for them, and re-layouts  15.3 us (7%)
  between operations  13.6 us (6%)
  other arithmetic  13.1 us (6%)
  matrix products  10.7 us (5%)
    all_gather x1, blocking collectives, per_device(): all_packed = lax.all_gather(packed, 'req', axis=0, tiled=True)  57.9 us
    all_gather x1, blocking collectives, per_device(): by_slot = lax.all_gather(normed, 'req', axis=0, tiled=True)  56.6 us
    all_to_all x1, blocking collectives, per_device(): lax.all_to_all(combined.reshape(req_count, per_dev, col_count), 'req', 0,...  27.2 us
    reduce_scatter x1, waiting for transfers between devices, per_device(): weighted = lax.psum_scatter(weighted, 'kv', scatter_dimension=1, tiled=True)  16.9 us
    psum x1, blocking collectives, per_device(): summed = lax.psum(summed_in, 'kv')  13.9 us
    unnamed x12, local copies, waits for them, and re-layouts  5.18 us
  transfers between devices with their start and end apart: 1, of which 1 were waited for; matrix products, arithmetic and copies ran while one was open for 0% of the time, Pallas kernels for 0%

commit v1 on v0

--- a/solution.py
+++ b/solution.py
@@ -84,7 +84,9 @@
     normed = (hidden * lax.rsqrt(squares / model_width + 1e-06)[:, None] * gain).astype(
         jnp.bfloat16
     )
-    by_slot = lax.all_gather(normed, "req", axis=0, tiled=True)
+    by_slot = jnp.concatenate(
+        lax.all_to_all(jnp.stack(lax.axis_size("req") * [normed]), "req", 0, 0), axis=0
+    )
     slot_of = (
         jnp.zeros((total_reqs,), jnp.int32)
         .at[slot_order]

time: 226 us -> 193 us (0.85)
  blocking collectives: 156 us -> 99 us
  waiting for transfers between devices: 17 us -> 29.6 us
  starting transfers between devices: 0.01 us -> 9.83 us
    all_gather x1 -> x0, blocking collectives: 56.6 us -> none  [per_device(): by_slot = lax.all_gather(normed, 'req', axis=0, tiled=True)]
    all_to_all x0 -> x1, waiting for transfers between devices: none -> 13.5 us  [per_device(): lax.all_to_all(jnp.stack(lax.axis_size('req') * [normed]), 'req', 0, 0)]
    all_to_all x0 -> x1, starting transfers between devices: none -> 9.79 us  [per_device(): lax.all_to_all(jnp.stack(lax.axis_size('req') * [normed]), 'req', 0, 0)]
    unnamed x12 -> x11, local copies, waits for them, and re-layouts: 5.18 us -> 2.46 us
    reshape x0 -> x1, local copies, waits for them, and re-layouts: none -> 2.71 us  [per_device(): jnp.concatenate(lax.all_to_all(jnp.stack(lax.axis_size('req') * [normed])...]
  transfers between devices with their start and end apart: 1 -> 2, of which waited for: 1 -> 2; matrix products, arithmetic and copies ran while one was open for 0% -> 3% of each run, Pallas kernels for 0% -> 0%
where the time goes in v1:
time: 193 us; the launch traced here: 192 us
  blocking collectives  99 us (51%)
  waiting for transfers between devices  29.6 us (15%)
  local copies, waits for them, and re-layouts  16.5 us (9%)
  between operations  13.6 us (7%)
  other arithmetic  13.1 us (7%)
  matrix products  10.7 us (6%)
  starting transfers between devices  9.83 us (5%)
    all_gather x1, blocking collectives, per_device(): all_packed = lax.all_gather(packed, 'req', axis=0, tiled=True)  57.9 us
    all_to_all x1, blocking collectives, per_device(): lax.all_to_all(combined.reshape(req_count, per_dev, col_count), 'req', 0,...  27.2 us
    reduce_scatter x1, waiting for transfers between devices, per_device(): weighted = lax.psum_scatter(weighted, 'kv', scatter_dimension=1, tiled=True)  16.1 us
    psum x1, blocking collectives, per_device(): summed = lax.psum(summed_in, 'kv')  13.9 us
    all_to_all x1, waiting for transfers between devices, per_device(): lax.all_to_all(jnp.stack(lax.axis_size('req') * [normed]), 'req', 0, 0)  13.5 us
    all_to_all x1, starting transfers between devices, per_device(): lax.all_to_all(jnp.stack(lax.axis_size('req') * [normed]), 'req', 0, 0)  9.79 us
    scatter-add x2, other arithmetic, per_device(): combined = jnp.zeros((total_reqs, col_count), jnp.float32).at[picked].add...  4.1 us
  transfers between devices with their start and end apart: 2, of which 2 were waited for; matrix products, arithmetic and copies ran while one was open for 3% of the time, Pallas kernels for 0%

profile of v1, /device:TPU:1, one launch (start us, length us, event | category | flops | bytes accessed | tf_op | source)
XLA Modules:
  0.0 192.3 jit_solution(15898165780690832009)
XLA Ops:
  6.5 0.9 compare_select_fusion.4
  8.7 57.9 %all-gather = bf16[64,2,1536]{2,1,0:T(2,128)(2,1)} all-gather(bf16[1,2,1536]{2,1,0:T(2,128)(2,1)S(1)} %maximum_bitcast_fusion), channel_id=1, replica_groups=mesh['req'=64,'kv'=4] {'req'}, dimensions={0}, use_global_device_ids=true | all-gather | bytes 399360 | tf_op jit(solution)/shard_map/all_gather | solution.py:38
  66.6 1.9 reshape.238
  68.5 1.6 gather_fusion.1
  70.2 1.3 gather_fusion
  71.7 2.3 %fusion.50 = (f32[2,5]{1,0:T(2,128)S(1)}, f32[2,5,4096]{2,1,0:T(8,128)S(1)}) fusion(bf16[2,5,128]{2,1,0:T(8,128)(2,1)S(1)} %reshape.156, bf16[2,4096,128]{2,1,0:T(8,128)(2,1)} %param.19, pred[2,4096]{1,0:T(4,128)(4,1)S(1)} %iota_compare_fusion), kind=kOutput, calls=%fused_computation.84 | convolution fusion | flops 10608630 | bytes 2271784 | tf_op jit(solution)/shard_map/rqd,rld->rql/dot_general | solution.py:48
  76.1 2.0 %fusion.16 = bf16[1,2,5,128]{3,2,1,0:T(8,128)(2,1)S(1)} fusion(bf16[2,4096,128]{2,1,0:T(8,128)(2,1)} %param.20, f32[2,5,4096]{2,1,0:T(8,128)S(1)} %get-tuple-element.16, f32[2,5]{1,0:T(2,128)S(1)} %multiply_maximum_fusion, f32[2,5]{1,0:T(2,128)} %get-tuple-element.14, f32[2,128]{1,0:T(2,128)S(1)} %get-tuple-element.11, f32[2,5]{1,0:T(2,128)} %convert_element_type.49), kind=kOutput, calls=%fused_computation.22 | convolution fusion | flops 10572800 | bytes 2264696 | tf_op jit(solution)/shard_map/rql,rld->rqd/dot_general | solution.py:61
  78.7 13.9 %psum.7 = f32[3,2560]{1,0:T(4,128)S(1)} all-reduce(f32[3,2560]{1,0:T(4,128)S(1)} %add_dynamic-update-slice_fusion), channel_id=1, replica_groups=mesh['req'=64,'kv'=4] {'kv'}, use_global_device_ids=true, to_apply=%region_7.8 | all-reduce | flops 7680 | bytes 61440 | tf_op jit(solution)/shard_map/psum | solution.py:80
  92.9 1.2 stack.2
  94.1 9.8 %all-to-all-start = ((bf16[64,2,2560]{2,1,0:T(2,128)(2,1)}), bf16[64,2,2560]{2,1,0:T(2,128)(2,1)}, u32[]{:S(2)}, u32[]{:S(2)}) async-start(bf16[64,2,2560]{2,1,0:T(2,128)(2,1)} %stack.2), calls=%async_computation | async-start | bytes 1310720 | tf_op jit(solution)/shard_map/all_to_all | solution.py:88
  104.4 1.4 scatter_custom_fusion
  106.6 1.0 scatter_custom_fusion.1
  107.6 0.8 fusion.32
  110.6 13.5 %all-to-all-done = bf16[64,2,2560]{2,1,0:T(2,128)(2,1)} async-done(((bf16[64,2,2560]{2,1,0:T(2,128)(2,1)}), bf16[64,2,2560]{2,1,0:T(2,128)(2,1)}, u32[]{:S(2)}, u32[]{:S(2)}) %all-to-all-start) | async-done | bytes 655392 | tf_op jit(solution)/shard_map/all_to_all | solution.py:88
  124.2 2.7 %reshape.158 = bf16[128,2560]{1,0:T(8,128)(2,1)} reshape(bf16[64,2,2560]{2,1,0:T(2,128)(2,1)} %all-to-all-done) | data formatting | bytes 1310720 | tf_op jit(solution)/shard_map/reshape | solution.py:87
  126.9 1.9 gather_fusion.3
  128.8 1.9 %fusion.4 = f32[24,384]{1,0:T(8,128)S(1)} fusion(bf16[24,2560]{1,0:T(8,128)(2,1)S(1)} %gather_fusion.3, bf16[1,2560,384]{2,1,0:T(8,128)(2,1)} %param.27), kind=kOutput, calls=%fused_computation.15 | convolution fusion | flops 47185920 | bytes 2125824 | tf_op jit(solution)/shard_map/dot_general | solution.py:104
  130.7 3.8 %convolution_multiply_fusion.1 = f32[24,2560]{1,0:T(8,128)} fusion(bf16[1,384,2560]{2,1,0:T(8,128)(2,1)} %param.29, bf16[24,2560]{1,0:T(8,128)(2,1)S(1)} %gather_fusion.3, bf16[1,2560,384]{2,1,0:T(8,128)(2,1)} %param.28, f32[24]{0:T(128)S(1)} %compare_select_fusion.5, f32[24,384]{1,0:T(8,128)S(1)} %fusion.4), kind=kOutput, calls=%fused_computation.11 | convolution fusion | flops 94488576 | bytes 4337760 | tf_op jit(solution)/shard_map/dot_general | solution.py:107
  134.5 16.1 %reduce-scatter.2.cloned.1.call-done = f32[24,640]{1,0:T(8,128)} async-done(((f32[24,2560]{1,0:T(8,128)}), f32[24,640]{1,0:T(8,128)}) %reduce-scatter.2.cloned.1.call-update) | async-done | bytes 61456 | tf_op jit(solution)/shard_map/reduce_scatter | solution.py:110
  150.6 1.7 scatter_custom_fusion.2
  152.3 2.4 %scatter_custom_fusion.3 = f32[128,640]{1,0:T(8,128)} fusion(f32[128,640]{1,0:T(8,128)} %scatter_custom_fusion.2, s32[2]{0:T(128)} %copy-done.3, f32[2,2560]{1,0:T(2,128)S(1)} %get-tuple-element.7, s32[]{:T(128)} %constant.31.clone.1, s32[]{:T(128)S(6)} %select_n.104), kind=kCustom, calls=%fused_computation.53 | custom fusion | flops 1280 | bytes 333316 | tf_op jit(solution)/shard_map/scatter-add | solution.py:117
  154.7 1.9 reshape.159
  156.6 27.2 %all_to_all.10 = f32[64,2,640]{2,1,0:T(2,128)} all-to-all(f32[64,2,640]{2,1,0:T(2,128)} %reshape.159), channel_id=1, replica_groups=mesh['req'=64,'kv'=4] {'req'}, dimensions={0} | all-to-all | bytes 655360 | tf_op jit(solution)/shard_map/all_to_all | solution.py:123
  183.8 1.7 reduce_sum.53
  (49 shorter events, 8.0 us)
Async XLA Ops:
  6.5 71.6 %copy-start = (bf16[640,2560]{1,0:T(8,128)(2,1)S(1)}, bf16[640,2560]{1,0:T(8,128)(2,1)}, u32[]{:S(2)}) copy-start(bf16[640,2560]{1,0:T(8,128)(2,1)} %param.23) | copy-start | bytes 9830404
  7.4 0.5 copy-start.3
  78.1 25.8 %copy-start.1 = (f32[128,6]{0,1:T(8,128)S(1)}, f32[128,6]{0,1:T(8,128)}, u32[]{:S(2)}) copy-start(f32[128,6]{0,1:T(8,128)} %param.26) | copy-start | bytes 9220
  78.1 25.8 %copy-start.2 = (s32[128,6]{0,1:T(8,128)S(1)}, s32[128,6]{0,1:T(8,128)}, u32[]{:S(2)}) copy-start(s32[128,6]{0,1:T(8,128)} %param.25) | copy-start | bytes 9220
  78.7 27.3 %copy-start.4 = (s32[128]{0:T(128)S(1)}, s32[128]{0:T(128)}, u32[]{:S(2)}) copy-start(s32[128]{0:T(128)} %param.22) | copy-start | bytes 1540
  94.1 30.1 %all-to-all-start = ((bf16[64,2,2560]{2,1,0:T(2,128)(2,1)}), bf16[64,2,2560]{2,1,0:T(2,128)(2,1)}, u32[]{:S(2)}, u32[]{:S(2)}) async-start(bf16[64,2,2560]{2,1,0:T(2,128)(2,1)} %stack.2), calls=%async_computation | async-start | bytes 1310720 | tf_op jit(solution)/shard_map/all_to_all | solution.py:88
  103.9 46.7 %reduce-scatter.2.cloned.1.call-start = ((), (), s32[]{:S(2)}) async-start(), calls=%async_computation.3 | async-start | bytes 307200 | tf_op jit(solution)/shard_map/reduce_scatter | solution.py:110
Sparse Core Ops, SparseCore 0:
  134.6 15.9 reduce-scatter.1
